TPU v7x, 256 devices: a whole 4x4x8 slice. The times are simulated.
256 devices in a mesh: blk: 32 (over x, y, core), row: 8 (over z).
Axes of the slice: x: 4, y: 4, z: 8, core: 2. Of those that a mesh axis runs over, the one named last changes fastest.
Arguments:
- samples: bfloat16 [1024, 8192], P('blk', 'row'), may hold values from -8 to 8, as said below
- blocks: int32 [64, 4], replicated, may hold values from 0 to 31
- factor: float32 [64, 1024], P(None, 'row'), may hold values from -1.2 to 1.2
Outputs:
- cumulants: float32 [64, 1024, 1024], P('blk', 'row')
- factor_out: float32 [64, 1024], P(None, 'row')
Inputs may be any that keep to these rules, and one draw needn't show every extreme that they name: `samples`: channel values are drawn with mean zero.
All inputs are finite; a program needn't handle non-finite values.
Results may differ from a plain program's by a relative error of at most 0.0014.
Values may be sent and summed in bfloat16 or wider, within the bound.
No kernel may reach another device: no remote copies, remote signals or barrier semaphores. Data moves between devices by JAX's collectives and lax.ppermute only.
A program may use at most 64 MiB of HBM per device.

v0:
```python
import jax
import jax.numpy as jnp
from jax import lax
from jax.sharding import PartitionSpec as P

CHANNELS = 1024
BLOCK = 32
RANK = 64
SAMPLES = 8192
ITERS = 2
step_size = 0.2


def pair_rows(left, right):
    product = left[:, None, :].astype(jnp.float32) * right[None, :, :].astype(jnp.float32)
    return product.reshape(left.shape[0] * right.shape[0], left.shape[1]).astype(jnp.bfloat16)


def contract_last(left, right):
    return lax.dot_general(
        left, right, (((1,), (1,)), ((), ())), preferred_element_type=jnp.float32
    )


def gauss_terms(gram, count, width, row_lo):
    highest = lax.Precision.HIGHEST

    def part(first, second):
        return gram[first * width : (first + 1) * width, second * width : (second + 1) * width]

    cov_ab = lax.dynamic_slice_in_dim(part(0, 1), row_lo, count, 0)
    cov_ac = lax.dynamic_slice_in_dim(part(0, 2), row_lo, count, 0)
    cov_ad = lax.dynamic_slice_in_dim(part(0, 3), row_lo, count, 0)
    cov_cd = part(2, 3)
    cov_bd = part(1, 3)
    cov_bc = part(1, 2)
    first_term = cov_ab.reshape(-1)[:, None] * cov_cd.reshape(-1)[None, :]
    second_term = jnp.einsum("ik,jl->ijkl", cov_ac, cov_bd, precision=highest).reshape(
        count * width, width * width
    )
    third_term = jnp.einsum("il,jk->ijkl", cov_ad, cov_bc, precision=highest).reshape(
        count * width, width * width
    )
    return first_term + second_term + third_term


def add_cols(total, piece, start):
    old = lax.dynamic_slice_in_dim(total, start, piece.shape[1], 1)
    return lax.dynamic_update_slice_in_dim(total, old + piece, start, 1)


def add_grads(total, kslab, full, ids, row_lo, count, width):
    highest = lax.Precision.HIGHEST
    rank = full.shape[0]
    start_a = ids[0] * width + row_lo
    fac_a = lax.dynamic_slice_in_dim(full, start_a, count, 1)
    fac_b = lax.dynamic_slice_in_dim(full, ids[1] * width, width, 1)
    fac_c = lax.dynamic_slice_in_dim(full, ids[2] * width, width, 1)
    fac_d = lax.dynamic_slice_in_dim(full, ids[3] * width, width, 1)
    upair = (fac_a[:, :, None] * fac_b[:, None, :]).reshape(rank, count * width)
    vpair = (fac_c[:, :, None] * fac_d[:, None, :]).reshape(rank, width * width)
    model = lax.dot_general(upair, vpair, (((0,), (0,)), ((), ())), precision=highest)
    resid = kslab - model
    wmat = lax.dot_general(vpair, resid, (((1,), (1,)), ((), ())), precision=highest).reshape(
        rank, count, width
    )
    zmat = jnp.dot(upair, resid, precision=highest).reshape(rank, width, width)
    total = add_cols(total, jnp.sum(wmat * fac_b[:, None, :], axis=2), start_a)
    total = add_cols(total, jnp.sum(wmat * fac_a[:, :, None], axis=1), ids[1] * width)
    total = add_cols(total, jnp.sum(zmat * fac_d[:, None, :], axis=2), ids[2] * width)
    total = add_cols(total, jnp.sum(zmat * fac_c[:, :, None], axis=1), ids[3] * width)
    return total


def gather_factor(columns):
    return lax.all_gather(columns, "row", axis=1, tiled=True)


def per_device(samples, blocks, factor):
    width = BLOCK
    row_count = lax.axis_size("row")
    count = width // row_count
    row_lo = lax.axis_index("row") * count
    per_owner = blocks.shape[0] // lax.axis_size("blk")
    mine = lax.dynamic_slice_in_dim(blocks, lax.axis_index("blk") * per_owner, per_owner, 0)
    needed = mine.reshape(-1)
    pairs = width * width
    piece = lax.all_gather(samples, "blk", axis=0, tiled=True)
    pieces = piece.shape[0] // width
    owned = jnp.arange(pieces, dtype=jnp.int32)
    select = (needed[:, None] == owned[None, :]).astype(jnp.bfloat16)
    shaped = piece.reshape(pieces, width, piece.shape[1])
    taken = jnp.einsum("mb,bcs->mcs", select, shaped, preferred_element_type=jnp.float32)
    local = taken.astype(jnp.bfloat16)
    slabs = []
    whole = lax.all_gather(local, "row", axis=2, tiled=True)
    sample_block = min(SAMPLES, 2048)
    for slot in range(per_owner):
        source_a = whole[4 * slot]
        source_b = whole[4 * slot + 1]
        source_c = whole[4 * slot + 2]
        source_d = whole[4 * slot + 3]

        def accumulate(index, moment):
            low = index * sample_block
            left = lax.dynamic_slice(source_a, (row_lo, low), (count, sample_block))
            right = lax.dynamic_slice_in_dim(source_b, low, sample_block, 1)
            third = lax.dynamic_slice_in_dim(source_c, low, sample_block, 1)
            fourth = lax.dynamic_slice_in_dim(source_d, low, sample_block, 1)
            pmat = pair_rows(left, right)
            qmat = pair_rows(third, fourth)
            return moment + contract_last(pmat, qmat)

        moment = lax.fori_loop(
            0, SAMPLES // sample_block, accumulate, jnp.zeros((count * width, pairs), jnp.float32)
        )
        moment = moment / SAMPLES
        joined = whole[4 * slot : 4 * slot + 4].reshape(4 * width, whole.shape[2])
        gram = contract_last(joined, joined) / SAMPLES
        slabs.append(moment - gauss_terms(gram, count, width, row_lo))
    columns = factor
    full = gather_factor(columns)
    for step in range(ITERS):
        grad = jnp.zeros(full.shape, jnp.float32)
        for slot in range(per_owner):
            grad = add_grads(grad, slabs[slot], full, mine[slot], row_lo, count, width)
        owned_cols = lax.psum_scatter(grad, "row", scatter_dimension=1, tiled=True)
        owned_cols = lax.psum(owned_cols, "blk")
        squares = lax.psum(jnp.sum(owned_cols * owned_cols), "row")
        scale = lax.rsqrt(squares / (RANK * CHANNELS) + 1e-06)
        columns = columns + step_size * scale * owned_cols
        if step + 1 < ITERS:
            full = gather_factor(columns)
    return (jnp.stack(slabs), columns)


def solution(mesh):
    placed = (P("blk", "row"), P(), P(None, "row"))
    return jax.shard_map(
        per_device,
        mesh=mesh,
        in_specs=placed,
        out_specs=(P("blk", "row", None), P(None, "row")),
        check_vma=False,
    )
```

profile of v0, /device:TPU:32, one launch (start us, length us, event | category | flops | bytes accessed | tf_op | source)
XLA Modules:
  0.0 646.9 jit_solution(17991353607669108797)
XLA Ops:
  8.2 53.5 %all-gather.3.cloned.1.call-done = bf16[1024,1024]{1,0:T(8,128)(2,1)} async-done(((bf16[32,1024]{1,0:T(8,128)(2,1)}), bf16[1024,1024]{1,0:T(8,128)(2,1)}) %all-gather.3.cloned.1.call-update) | async-done | bytes 2097168 | tf_op jit(solution)/shard_map/all_gather | solution.py:88
  61.8 4.7 fusion.2
  72.3 26.5 %all_gather.14 = f32[64,1024]{1,0:T(8,128)S(1)} all-gather(f32[64,128]{1,0:T(8,128)S(1)} %copy-done.11), channel_id=1, replica_groups=mesh['blk'=32,'row'=8] {'row'}, dimensions={1}, use_global_device_ids=true | all-gather | bytes 294912 | tf_op jit(solution)/shard_map/all_gather | solution.py:76
  101.3 19.8 %all-gather.5.cloned.1.call-done = bf16[8,32,8192]{2,0,1:T(8,128)(2,1)} async-done(((bf16[8,32,1024]{2,0,1:T(8,128)(2,1)}), bf16[8,32,8192]{2,0,1:T(8,128)(2,1)}) %all-gather.5.cloned.1.call-update) | async-done | bytes 4194320 | tf_op jit(solution)/shard_map/all_gather | solution.py:96
  121.1 21.7 %fusion.10 = (bf16[1,32,8192]{2,0,1:T(2,128)(2,1)S(1)}, bf16[1,32,8192]{2,0,1:T(2,128)(2,1)}, bf16[1,32,8192]{2,0,1:T(2,128)(2,1)}, bf16[1,32,8192]{2,0,1:T(2,12...) fusion(bf16[8,32,8192]{2,0,1:T(8,128)(2,1)} %all-gather.5.clone, ...), kind=kLoop, calls=%fused_computation.112 | loop fusion | bytes 8388608 | tf_op jit(solution)/shard_map/slice | solution.py:102
  145.9 31.4 %while.32 = (s32[]{:T(128)}, f32[128,1024]{1,0:T(8,128)S(1)}, bf16[32,8192]{1,0:T(8,128)(2,1)}, s32[]{:T(128)}, bf16[32,8192]{1,0:T(8,128)(2,1)S(1)}, /*index=5*...) while((s32[]{:T(128)}, f32[128,1024]{1,0:T(8,128)S(1)}, ...), condition=%wide.region_1.0_spmd.clone, body=%wide.region_0.0_spmd.clone.sunk | while | flops 542056448 | bytes 12533941 | solution.py:114
  150.0 3.8 convolution_add_fusion.4
  157.9 3.8 convolution_add_fusion.4
  165.7 3.8 convolution_add_fusion.4
  173.6 3.8 convolution_add_fusion.4
  177.4 6.7 %fusion.11 = (bf16[4,32,8192]{2,0,1:T(4,128)(2,1)S(1)}, bf16[4,32,8192]{2,0,1:T(4,128)(2,1)}) fusion(bf16[8,32,8192]{2,0,1:T(8,128)(2,1)} %all-gather.5.cloned.1.call-done), kind=kLoop, calls=%fused_computation.113 | loop fusion | bytes 8388608 | tf_op jit(solution)/shard_map/slice | solution.py:118
  197.6 3.6 copy_bitcast_fusion.2
  203.3 35.3 %while.33 = (s32[]{:T(128)}, f32[128,1024]{1,0:T(8,128)S(1)}, bf16[32,8192]{1,0:T(8,128)(2,1)}, s32[]{:T(128)}, bf16[32,8192]{1,0:T(8,128)(2,1)S(1)}, /*index=5*...) while((s32[]{:T(128)}, f32[128,1024]{1,0:T(8,128)S(1)}, ...), condition=%wide.region_3.0_spmd.clone, body=%wide.region_2.0_spmd.clone.sunk | while | flops 542056448 | bytes 12533941 | solution.py:114
  208.2 3.8 convolution_add_fusion.5
  217.0 3.8 convolution_add_fusion.5
  225.8 3.8 convolution_add_fusion.5
  234.6 3.8 convolution_add_fusion.5
  250.8 37.1 %reduce-scatter.3.cloned.1.call-done = f32[64,128]{0,1:T(8,128)} async-done(((f32[64,1024]{0,1:T(8,128)}), f32[64,128]{0,1:T(8,128)}) %reduce-scatter.3.cloned.1.call-update) | async-done | bytes 32784 | tf_op jit(solution)/shard_map/reduce_scatter | solution.py:127
  287.9 124.3 %psum.28 = f32[64,128]{0,1:T(8,128)S(1)} all-reduce(f32[64,128]{0,1:T(8,128)} %reduce-scatter.3.cloned.1.call-done), channel_id=1, replica_groups=mesh['blk'=32,'row'=8] {'blk'}, use_global_device_ids=true, to_apply=%region_13.0 | all-reduce | flops 8192 | bytes 65536 | tf_op jit(solution)/shard_map/psum | solution.py:128
  412.9 16.0 %psum.29 = f32[]{:T(128)} all-reduce(f32[]{:T(128)} %multiply_reduce_fusion.13), channel_id=1, replica_groups=mesh['blk'=32,'row'=8] {'row'}, use_global_device_ids=true, to_apply=%region_15.0 | all-reduce | flops 1 | bytes 8 | tf_op jit(solution)/shard_map/psum | solution.py:129
  429.7 24.3 %all_gather.15 = f32[64,1024]{0,1:T(8,128)S(1)} all-gather(f32[64,128]{0,1:T(8,128)S(1)} %multiply_add_fusion.1), channel_id=1, replica_groups=mesh['blk'=32,'row'=8] {'row'}, dimensions={1}, use_global_device_ids=true | all-gather | bytes 294912 | tf_op jit(solution)/shard_map/all_gather | solution.py:76
  463.1 34.0 %reduce-scatter.5.cloned.1.call-done = f32[64,128]{0,1:T(8,128)} async-done(((f32[64,1024]{0,1:T(8,128)}), f32[64,128]{0,1:T(8,128)}) %reduce-scatter.5.cloned.1.call-update) | async-done | bytes 32784 | tf_op jit(solution)/shard_map/reduce_scatter | solution.py:127
  497.1 124.3 %psum.30 = f32[64,128]{0,1:T(8,128)S(1)} all-reduce(f32[64,128]{0,1:T(8,128)} %reduce-scatter.5.cloned.1.call-done), channel_id=1, replica_groups=mesh['blk'=32,'row'=8] {'blk'}, use_global_device_ids=true, to_apply=%region_25.0 | all-reduce | flops 8192 | bytes 65536 | tf_op jit(solution)/shard_map/psum | solution.py:128
  623.1 15.9 %psum.31 = f32[]{:T(128)} all-reduce(f32[]{:T(128)} %multiply_reduce_fusion.8), channel_id=1, replica_groups=mesh['blk'=32,'row'=8] {'row'}, use_global_device_ids=true, to_apply=%region_27.0 | all-reduce | flops 1 | bytes 8 | tf_op jit(solution)/shard_map/psum | solution.py:129
  (167 shorter events, 82.9 us)
Async XLA Ops:
  7.2 0.8 copy-start
  7.2 65.1 %copy-start.11 = (f32[64,128]{1,0:T(8,128)S(1)}, f32[64,128]{1,0:T(8,128)}, u32[]{:S(2)}) copy-start(f32[64,128]{1,0:T(8,128)} %param.9) | copy-start | bytes 98308
  7.2 54.6 %all-gather.3.cloned.1.call-start = ((), (), s32[]{:S(2)}) async-start(), calls=%async_computation.2 | async-start | bytes 2162688 | tf_op jit(solution)/shard_map/all_gather | solution.py:88
  7.9 113.2 %all-gather.5.cloned.1.call-start = ((), (), s32[]{:S(2)}) async-start(), calls=%async_computation.3 | async-start | bytes 4718592 | tf_op jit(solution)/shard_map/all_gather | solution.py:96
  66.5 221.4 %reduce-scatter.3.cloned.1.call-start = ((), (), s32[]{:S(2)}) async-start(), calls=%async_computation.4 | async-start | bytes 589824 | tf_op jit(solution)/shard_map/reduce_scatter | solution.py:127
  192.3 2.1 copy-start.12
  194.4 1.5 copy-start.2
  196.5 4.6 copy-start.4
  196.5 4.6 copy-start.6
  197.6 3.6 copy-start.7
  242.8 1.5 copy-start.1
  244.3 3.4 copy-start.3
  244.3 3.4 copy-start.5
  245.9 3.3 copy-start.10
  249.9 0.8 copy-start.9
  250.7 246.3 %reduce-scatter.5.cloned.1.call-start = ((), (), s32[]{:S(2)}) async-start(), calls=%async_computation.5 | async-start | bytes 589824 | tf_op jit(solution)/shard_map/reduce_scatter | solution.py:127
  462.3 0.8 copy-start.8
Sparse Core Ops, SparseCore 0:
  10.6 51.1 all-gather.2
  66.6 54.4 all-gather.4
  250.8 36.9 reduce-scatter.2
  463.2 33.8 reduce-scatter.4
where the time goes:
time: 648 us; the launch traced here: 647 us
  blocking collectives  331 us (51%)
  waiting for transfers between devices  145 us (22%)
  local copies, waits for them, and re-layouts  57.5 us (9%)
  matrix products  47.2 us (7%)
  other arithmetic  44.2 us (7%)
  between operations  20.7 us (3%)
    psum x2, blocking collectives, per_device(): owned_cols = lax.psum(owned_cols, 'blk')  249 us
    reduce_scatter x2, waiting for transfers between devices, per_device(): owned_cols = lax.psum_scatter(grad, 'row', scatter_dimension=1, tiled=True)  71.1 us
    all_gather x1, waiting for transfers between devices, per_device(): piece = lax.all_gather(samples, 'blk', axis=0, tiled=True)  53.5 us
    all_gather x2, blocking collectives, gather_factor(): return lax.all_gather(columns, 'row', axis=1, tiled=True)  50.7 us
    psum x2, blocking collectives, per_device(): squares = lax.psum(jnp.sum(owned_cols * owned_cols), 'row')  32 us
    dot_general x10, matrix products, contract_last(): lax.dot_general(left, right, (((1,), (1,)), ((), ())), preferred_element_...  31.6 us
    convert_element_type x16, other arithmetic, pair_rows(): product.reshape(left.shape[0] * right.shape[0], left.shape[1])  24.8 us
    slice x1, local copies, waits for them, and re-layouts, per_device(): source_d = whole[4 * slot + 3]  21.7 us
  transfers between devices with their start and end apart: 4, of which 4 were waited for; matrix products, arithmetic and copies ran while one was open for 1% of the time, Pallas kernels for 0%

commit v1 on v0

--- a/solution.py
+++ b/solution.py
@@ -2,6 +2,7 @@
 import jax.numpy as jnp
 from jax import lax
 from jax.sharding import PartitionSpec as P
+from jax.lax import axis_index, axis_size, ppermute
 
 CHANNELS = 1024
 BLOCK = 32
@@ -9,6 +10,12 @@
 SAMPLES = 8192
 ITERS = 2
 step_size = 0.2
+
+
+def counts_read(inputs, dimension_no):
+    a_next = list(inputs.shape[1:])
+    a_next[dimension_no] *= inputs.shape[0]
+    return jnp.moveaxis(inputs, 0, dimension_no).reshape(a_next)
 
 
 def pair_rows(left, right):
@@ -73,7 +80,25 @@
 
 
 def gather_factor(columns):
-    return lax.all_gather(columns, "row", axis=1, tiled=True)
+
+    def ways_start(panel, ax_name, out_dim):
+        k_all = axis_size(ax_name)
+        heap = [(t, (t + 1) % k_all) for t in range(k_all)]
+        state_next, mid_arr = ([], [])
+        tick = 0
+        kept_rows = [(k0, dev_i) for dev_i, k0 in heap]
+        while tick < k_all - 1:
+            if tick % 2 == 0:
+                state_next.append(ppermute(state_next[-1] if state_next else panel, ax_name, heap))
+            else:
+                mid_arr.append(ppermute(mid_arr[-1] if mid_arr else panel, ax_name, perm=kept_rows))
+            tick = tick + 1
+        main = jnp.stack([*state_next[::-1], panel, *mid_arr])
+        reply = axis_index(ax_name) - len(state_next)
+        main = main[(jnp.arange(k_all) - reply) % k_all]
+        return counts_read(main, out_dim)
+
+    return ways_start(columns, "row", 1)
 
 
 def per_device(samples, blocks, factor):

time: 648 us -> 652 us (level)
  blocking collectives: 331 us -> 281 us
  waiting for transfers between devices: 145 us -> 172 us
  starting transfers between devices: 0.16 us -> 20.3 us
    all_gather x2 -> x0, blocking collectives: 50.7 us -> none  [gather_factor(): return lax.all_gather(columns, 'row', axis=1, tiled=True)]
    ppermute x0 -> x14, waiting for transfers between devices: none -> 21.9 us  [the longest x8 15.7 us: ways_start(): ppermute(state_next[-1] if state_next else panel, ax_name, heap)]
    ppermute x0 -> x14, starting transfers between devices: none -> 20.1 us  [the longest x6 11.6 us: ways_start(): ppermute(mid_arr[-1] if mid_arr else panel, ax_name, perm=kept_rows)]
  transfers between devices with their start and end apart: 4 -> 18, of which waited for: 4 -> 15; matrix products, arithmetic and copies ran while one was open for 1% -> 1% of each run, Pallas kernels for 0% -> 0%
where the time goes in v1:
time: 652 us; the launch traced here: 645 us
  blocking collectives  281 us (43%)
  waiting for transfers between devices  172 us (26%)
  local copies, waits for them, and re-layouts  59 us (9%)
  matrix products  48.1 us (7%)
  other arithmetic  43 us (7%)
  between operations  21.1 us (3%)
  starting transfers between devices  20.3 us (3%)
    psum x2, blocking collectives, per_device(): owned_cols = lax.psum(owned_cols, 'blk')  249 us
    reduce_scatter x2, waiting for transfers between devices, per_device(): owned_cols = lax.psum_scatter(grad, 'row', scatter_dimension=1, tiled=True)  72.3 us
    all_gather x1, waiting for transfers between devices, per_device(): piece = lax.all_gather(samples, 'blk', axis=0, tiled=True)  53.5 us
    psum x2, blocking collectives, per_device(): squares = lax.psum(jnp.sum(owned_cols * owned_cols), 'row')  31.9 us
    dot_general x10, matrix products, contract_last(): lax.dot_general(left, right, (((1,), (1,)), ((), ())), preferred_element_...  31.6 us
    convert_element_type x16, other arithmetic, pair_rows(): product.reshape(left.shape[0] * right.shape[0], left.shape[1])  24.8 us
    all_gather x1, waiting for transfers between devices, per_device(): whole = lax.all_gather(local, 'row', axis=2, tiled=True)  23.5 us
    slice x1, local copies, waits for them, and re-layouts, per_device(): source_d = whole[4 * slot + 3]  21.7 us
  transfers between devices with their start and end apart: 18, of which 15 were waited for; matrix products, arithmetic and copies ran while one was open for 1% of the time, Pallas kernels for 0%

profile of v1, /device:TPU:32, one launch (start us, length us, event | category | flops | bytes accessed | tf_op | source)
XLA Modules:
  0.0 644.7 jit_solution(1119086741036612326)
XLA Ops:
  8.2 53.5 %all-gather.3.cloned.1.call-done = bf16[1024,1024]{1,0:T(8,128)(2,1)} async-done(((bf16[32,1024]{1,0:T(8,128)(2,1)}), bf16[1024,1024]{1,0:T(8,128)(2,1)}) %all-gather.3.cloned.1.call-update) | async-done | bytes 2097168 | tf_op jit(solution)/shard_map/all_gather | solution.py:113
  61.8 4.7 fusion.2
  88.8 4.6 collective-permute-done.6
  96.6 23.5 %all-gather.5.cloned.1.call-done = bf16[8,32,8192]{2,0,1:T(8,128)(2,1)} async-done(((bf16[8,32,1024]{2,0,1:T(8,128)(2,1)}), bf16[8,32,8192]{2,0,1:T(8,128)(2,1)}) %all-gather.5.cloned.1.call-update) | async-done | bytes 4194320 | tf_op jit(solution)/shard_map/all_gather | solution.py:121
  120.1 21.7 %fusion.12 = (bf16[1,32,8192]{2,0,1:T(2,128)(2,1)}, bf16[1,32,8192]{2,0,1:T(2,128)(2,1)S(1)}, bf16[1,32,8192]{2,0,1:T(2,128)(2,1)S(1)}, bf16[1,32,8192]{2,0,1:T(...) fusion(bf16[8,32,8192]{2,0,1:T(8,128)(2,1)} %all-gather.5.clone, ...), kind=kLoop, calls=%fused_computation.138 | loop fusion | bytes 8388608 | tf_op jit(solution)/shard_map/slice | solution.py:127
  144.9 31.4 %while.33 = (s32[]{:T(128)}, f32[128,1024]{1,0:T(8,128)S(1)}, bf16[32,8192]{1,0:T(8,128)(2,1)}, s32[]{:T(128)}, bf16[32,8192]{1,0:T(8,128)(2,1)S(1)}, /*index=5*...) while((s32[]{:T(128)}, f32[128,1024]{1,0:T(8,128)S(1)}, ...), condition=%wide.region_3.0_spmd.clone, body=%wide.region_2.0_spmd.clone.sunk | while | flops 542056448 | bytes 12533941 | solution.py:139
  148.9 3.8 convolution_add_fusion.5
  156.8 3.8 convolution_add_fusion.5
  164.7 3.8 convolution_add_fusion.5
  172.5 3.8 convolution_add_fusion.5
  176.3 6.8 %fusion.13 = (bf16[4,32,8192]{2,0,1:T(4,128)(2,1)}, bf16[4,32,8192]{2,0,1:T(4,128)(2,1)S(1)}) fusion(bf16[8,32,8192]{2,0,1:T(8,128)(2,1)} %all-gather.5.cloned.1.call-done), kind=kLoop, calls=%fused_computation.139 | loop fusion | bytes 8388608 | tf_op jit(solution)/shard_map/slice | solution.py:143
  195.5 3.6 copy_bitcast_fusion.6
  201.3 35.3 %while.32 = (s32[]{:T(128)}, f32[128,1024]{1,0:T(8,128)S(1)}, bf16[32,8192]{1,0:T(8,128)(2,1)}, s32[]{:T(128)}, bf16[32,8192]{1,0:T(8,128)(2,1)S(1)}, /*index=5*...) while((s32[]{:T(128)}, f32[128,1024]{1,0:T(8,128)S(1)}, ...), condition=%wide.region_1.0_spmd.clone, body=%wide.region_0.0_spmd.clone.sunk | while | flops 542056448 | bytes 12533941 | solution.py:139
  206.2 3.8 convolution_add_fusion.4
  215.0 3.8 convolution_add_fusion.4
  223.8 3.8 convolution_add_fusion.4
  232.6 3.8 convolution_add_fusion.4
  249.7 37.5 %reduce-scatter.3.cloned.1.call-done = f32[64,128]{0,1:T(8,128)} async-done(((f32[64,1024]{0,1:T(8,128)}), f32[64,128]{0,1:T(8,128)}) %reduce-scatter.3.cloned.1.call-update) | async-done | bytes 32784 | tf_op jit(solution)/shard_map/reduce_scatter | solution.py:152
  287.2 124.3 %psum.28 = f32[64,128]{0,1:T(8,128)S(1)} all-reduce(f32[64,128]{0,1:T(8,128)} %reduce-scatter.3.cloned.1.call-done), channel_id=1, replica_groups=mesh['blk'=32,'row'=8] {'blk'}, use_global_device_ids=true, to_apply=%region_13.14 | all-reduce | flops 8192 | bytes 65536 | tf_op jit(solution)/shard_map/psum | solution.py:153
  412.3 15.9 %psum.29 = f32[]{:T(128)} all-reduce(f32[]{:T(128)} %multiply_reduce_fusion.13), channel_id=1, replica_groups=mesh['blk'=32,'row'=8] {'row'}, use_global_device_ids=true, to_apply=%region_15.16 | all-reduce | flops 1 | bytes 8 | tf_op jit(solution)/shard_map/psum | solution.py:154
  429.9 3.4 collective-permute-done.7
  459.8 34.8 %reduce-scatter.5.cloned.1.call-done = f32[64,128]{0,1:T(8,128)} async-done(((f32[64,1024]{0,1:T(8,128)}), f32[64,128]{0,1:T(8,128)}) %reduce-scatter.5.cloned.1.call-update) | async-done | bytes 32784 | tf_op jit(solution)/shard_map/reduce_scatter | solution.py:152
  494.5 124.3 %psum.30 = f32[64,128]{0,1:T(8,128)S(1)} all-reduce(f32[64,128]{0,1:T(8,128)} %reduce-scatter.5.cloned.1.call-done), channel_id=1, replica_groups=mesh['blk'=32,'row'=8] {'blk'}, use_global_device_ids=true, to_apply=%region_25.26 | all-reduce | flops 8192 | bytes 65536 | tf_op jit(solution)/shard_map/psum | solution.py:153
  620.5 16.0 %psum.31 = f32[]{:T(128)} all-reduce(f32[]{:T(128)} %multiply_reduce_fusion.8), channel_id=1, replica_groups=mesh['blk'=32,'row'=8] {'row'}, use_global_device_ids=true, to_apply=%region_27.28 | all-reduce | flops 1 | bytes 8 | tf_op jit(solution)/shard_map/psum | solution.py:154
  (214 shorter events, 118.1 us)
Async XLA Ops:
  7.2 59.4 %copy-start.12 = (f32[64,128]{1,0:T(8,128)S(1)}, f32[64,128]{1,0:T(8,128)}, u32[]{:S(2)}) copy-start(f32[64,128]{1,0:T(8,128)} %param.9) | copy-start | bytes 98308
  7.2 54.6 %all-gather.3.cloned.1.call-start = ((), (), s32[]{:S(2)}) async-start(), calls=%async_computation.2 | async-start | bytes 2162688 | tf_op jit(solution)/shard_map/all_gather | solution.py:113
  7.9 112.1 %all-gather.5.cloned.1.call-start = ((), (), s32[]{:S(2)}) async-start(), calls=%async_computation.3 | async-start | bytes 4718592 | tf_op jit(solution)/shard_map/all_gather | solution.py:121
  66.5 220.7 %reduce-scatter.3.cloned.1.call-start = ((), (), s32[]{:S(2)}) async-start(), calls=%async_computation.4 | async-start | bytes 589824 | tf_op jit(solution)/shard_map/reduce_scatter | solution.py:152
  66.6 4.0 collective-permute-start
  68.2 7.8 %collective-permute-start.4 = (f32[64,128]{1,0:T(8,128)S(1)}, f32[64,128]{1,0:T(8,128)S(1)}, u32[]{:S(2)}, u32[]{:S(2)}) collective-permute-start(f32[64,128]{1,0:T(8,128)S(1)} %copy-done.12), channel_id=1, source_target_pairs={{1,0},{2,1},{3,2},{4,3},{5,4},{6,5},{7,6},{0,7},{9,8},{10,9},{11,1... | collective-permute-start | bytes 98312 | tf_op jit(solution)/shard_map/ppermute | solution.py:94
  70.6 3.9 collective-permute-start.1
  74.5 5.3 collective-permute-start.2
  76.0 10.4 %collective-permute-start.5 = (f32[64,128]{1,0:T(8,128)S(1)}, f32[64,128]{1,0:T(8,128)S(1)}, u32[]{:S(2)}, u32[]{:S(2)}) collective-permute-start(f32[64,128]{1,0:T(8,128)S(1)} %collective-permute-done.4), channel_id=1, source_target_pairs={{1,0},{2,1},{3,2},{4,3},{5,4},{6,5},{7,6},{0,7},{9,8},{10,9},{11,1... | collective-permute-start | bytes 98312 | tf_op jit(solution)/shard_map/ppermute | solution.py:94
  79.8 8.9 %collective-permute-start.3 = (f32[64,128]{1,0:T(8,128)S(1)}, f32[64,128]{1,0:T(8,128)S(1)}, u32[]{:S(2)}, u32[]{:S(2)}) collective-permute-start(f32[64,128]{1,0:T(8,128)S(1)} %collective-permute-done.2), channel_id=1, source_target_pairs={{0,1},{1,2},{2,3},{3,4},{4,5},{5,6},{6,7},{7,0},{8,9},{9,10},{10,1... | collective-permute-start | bytes 98312 | tf_op jit(solution)/shard_map/ppermute | solution.py:92
  86.4 6.9 %collective-permute-start.6 = (f32[64,128]{1,0:T(8,128)S(1)}, f32[64,128]{1,0:T(8,128)S(1)}, u32[]{:S(2)}, u32[]{:S(2)}) collective-permute-start(f32[64,128]{1,0:T(8,128)S(1)} %collective-permute-done.5), channel_id=1, source_target_pairs={{1,0},{2,1},{3,2},{4,3},{5,4},{6,5},{7,6},{0,7},{9,8},{10,9},{11,1... | collective-permute-start | bytes 98312 | tf_op jit(solution)/shard_map/ppermute | solution.py:94
  194.5 4.6 copy-start.4
  194.5 4.6 copy-start.6
  195.5 3.6 copy-start.7
  242.3 3.3 copy-start.3
  242.3 3.3 copy-start.5
  249.7 244.9 %reduce-scatter.5.cloned.1.call-start = ((), (), s32[]{:S(2)}) async-start(), calls=%async_computation.5 | async-start | bytes 589824 | tf_op jit(solution)/shard_map/reduce_scatter | solution.py:152
  428.9 4.3 collective-permute-start.7
  433.3 4.8 collective-permute-start.8
  434.2 4.3 collective-permute-start.11
  438.1 5.5 collective-permute-start.9
  438.5 5.8 collective-permute-start.12
  443.6 5.5 collective-permute-start.10
  444.3 5.7 collective-permute-start.13
  (7 other events, 7.3 us)
Sparse Core Ops, SparseCore 0:
  10.6 51.1 all-gather.2
  66.6 53.3 all-gather.4
  249.8 37.3 reduce-scatter.2
  459.9 34.5 reduce-scatter.4
